TPU v7x, 256 devices: a whole 4x4x8 slice. The times are simulated.
256 devices in a mesh: tm: 4 (over y), row: 4 (over x), col: 16 (over z, core).
Axes of the slice: x: 4, y: 4, z: 8, core: 2. Of those that a mesh axis runs over, the one named last changes fastest.
Arguments:
- day_block: float32 [4, 4, 16, 32, 4, 4, 128], P('tm', None, 'col', None, None, 'row'), as said below
- left_coupling: float32 [4, 4, 16, 32, 4, 4, 128], P('tm', None, 'col', None, None, 'row'), may hold values from -0.125 to 0.125
- right_coupling: float32 [4, 4, 16, 32, 4, 4, 128], P('tm', None, 'col', None, None, 'row'), may hold values from -0.125 to 0.125
- separator_block: float32 [4, 4, 16, 32, 4, 4, 128], P('tm', None, 'col', None, None, 'row')
- arrow_coupling: float32 [4, 4, 16, 32, 64], P('tm', None, 'col'), may hold values from -0.125 to 0.125
- arrow_block: float32 [64, 64], replicated
Outputs:
- day_factor: float32 [4, 4, 16, 32, 4, 4, 128], P('tm', None, 'col', None, None, 'row')
- left_factor: float32 [4, 4, 16, 32, 4, 4, 128], P('tm', None, 'col', None, None, 'row')
- right_factor: float32 [4, 4, 16, 32, 4, 4, 128], P('tm', None, 'col', None, None, 'row')
- arrow_factor: float32 [4, 4, 16, 32, 64], P('tm', None, 'col')
- separator: float32 [4, 4, 16, 32, 4, 4, 128], P('tm', None, 'col', None, None, 'row')
- arrowhead: float32 [64, 64], replicated
Inputs may be any that keep to these rules, and one draw needn't show every extreme that they name: Each group's day_block and separator_block, and arrow_block, is an exactly symmetric matrix with all eigenvalues at least 1.
All inputs are finite; a program needn't handle non-finite values.
Results may differ from a plain program's by a relative error of at most 0.0001.
Values sent between devices are 32-bit elements; how exact they have to be, the bound alone decides.
No kernel may reach another device: no remote copies, remote signals or barrier semaphores. Data moves between devices by JAX's collectives and lax.ppermute only.
A program may use at most 128 MiB of HBM per device.

v0:
```python
import jax
import jax.numpy as jnp
from jax import lax
from jax.sharding import PartitionSpec as P


def passed_along(value, axis, steps):
    count = lax.axis_size(axis)
    initial, last = (max(0, -steps), min(count, count - steps))
    return lax.ppermute(value, axis, [(source, source + steps) for source in range(initial, last)])


def product(left, right):
    return jnp.dot(left, right, precision=lax.Precision.HIGHEST, preferred_element_type=jnp.float32)


def lower_inverse(factor):
    identity = jnp.eye(factor.shape[0], dtype=jnp.float32)
    return lax.linalg.triangular_solve(factor, identity, left_side=True, lower=True)


def reorder_nodes(whole, panels, col_width):
    count = whole.shape[0]
    col_count = lax.axis_size("col")
    spread = whole.reshape(count, panels, col_count, col_width)
    return jnp.transpose(spread, (2, 1, 3, 0)).reshape(col_count * panels * col_width, count)


def separator_term(solved, panels, col_width, row_width):
    whole = lax.all_gather(
        solved.reshape(solved.shape[0], panels, 1, row_width), "row", axis=2, tiled=True
    )
    ordered = reorder_nodes(whole, panels, col_width)
    return lax.psum_scatter(product(ordered, solved), "col", scatter_dimension=0, tiled=True)


def per_device(
    day_block, left_coupling, right_coupling, separator_block, arrow_coupling, arrow_block
):
    panels = day_block.shape[1]
    col_width = day_block.shape[3]
    row_width = day_block.shape[6]
    panel_size = col_width * lax.axis_size("col")
    arrow_rows = arrow_block.shape[0]
    col_index = lax.axis_index("col")
    row_index = lax.axis_index("row")
    matrix = day_block.reshape(panels, col_width, panels, row_width)
    left_part = left_coupling.reshape(panels, col_width, panels, row_width)
    right_part = right_coupling.reshape(panels, col_width, panels, row_width)
    arrow_part = arrow_coupling.reshape(panels, col_width, arrow_rows)
    rows_at = col_index * col_width + lax.broadcasted_iota(jnp.int32, (col_width, row_width), 0)
    cols_at = row_index * row_width + lax.broadcasted_iota(jnp.int32, (col_width, row_width), 1)
    factor_blocks = []
    left_blocks = []
    right_blocks = []
    arrow_blocks = []
    for current in range(panels):
        remain = panels - current
        gathered_day, gathered_left, gathered_right, gathered_arrow = (
            lax.all_gather(matrix[current, :, current:, :], "col", axis=0, tiled=True),
            lax.all_gather(left_part[current], "col", axis=0, tiled=True),
            lax.all_gather(right_part[current], "col", axis=0, tiled=True),
            lax.all_gather(arrow_part[current], "col", axis=0, tiled=True),
        )
        diagonal_full = lax.all_gather(gathered_day[:, 0:1, :], "row", axis=1, tiled=True).reshape(
            panel_size, panel_size
        )
        factor = jnp.linalg.cholesky(diagonal_full)
        inverse = lower_inverse(factor)
        owned = product(inverse, gathered_day.reshape(panel_size, remain * row_width)).reshape(
            panel_size, remain, row_width
        )
        if remain > 1:
            later = lax.all_gather(owned[:, 1:, None, :], "row", axis=2, tiled=True).reshape(
                panel_size, remain - 1, panel_size
            )
        solved_left = product(inverse, gathered_left.reshape(panel_size, panels * row_width))
        solved_right = product(inverse, gathered_right.reshape(panel_size, panels * row_width))
        solved_arrow = product(inverse, gathered_arrow)
        mine_rows = lax.dynamic_slice_in_dim(owned, col_index * col_width, col_width, 0)
        diagonal_part = jnp.where(cols_at >= rows_at, mine_rows[:, 0, :], 0.0)
        factor_blocks.append(
            jnp.concatenate(
                [
                    jnp.zeros((col_width, current, row_width), jnp.float32),
                    diagonal_part[:, None, :],
                    mine_rows[:, 1:, :],
                ],
                axis=1,
            )
        )
        left_blocks.append(
            lax.dynamic_slice_in_dim(solved_left, col_index * col_width, col_width, 0)
        )
        right_blocks.append(
            lax.dynamic_slice_in_dim(solved_right, col_index * col_width, col_width, 0)
        )
        arrow_blocks.append(
            lax.dynamic_slice_in_dim(solved_arrow, col_index * col_width, col_width, 0)
        )
        if remain > 1:
            mine_later = lax.dynamic_slice_in_dim(later, col_index * col_width, col_width, 2)
            mine_later = mine_later.reshape(panel_size, (remain - 1) * col_width).T
            owned_later = owned[:, 1:, :].reshape(panel_size, (remain - 1) * row_width)
            matrix = matrix.at[current + 1 :, :, current + 1 :, :].add(
                -product(mine_later, owned_later).reshape(
                    remain - 1, col_width, remain - 1, row_width
                )
            )
            left_part = left_part.at[current + 1 :].add(
                -product(mine_later, solved_left).reshape(remain - 1, col_width, panels, row_width)
            )
            right_part = right_part.at[current + 1 :].add(
                -product(mine_later, solved_right).reshape(remain - 1, col_width, panels, row_width)
            )
            arrow_part = arrow_part.at[current + 1 :].add(
                -product(mine_later, solved_arrow).reshape(remain - 1, col_width, arrow_rows)
            )
    day_factor = jnp.stack(factor_blocks).reshape(day_block.shape)
    left_solved = jnp.stack(left_blocks).reshape(panels * col_width, panels * row_width)
    right_solved = jnp.stack(right_blocks).reshape(panels * col_width, panels * row_width)
    arrow_solved = jnp.stack(arrow_blocks).reshape(panels * col_width, arrow_rows)
    separator_local = separator_block.reshape(panels * col_width, panels * row_width)
    right_term = separator_term(right_solved, panels, col_width, row_width)
    left_term = separator_term(left_solved, panels, col_width, row_width)
    from_next = passed_along(left_term, "tm", -1)
    separator = separator_local - right_term - from_next
    arrow_local = product(arrow_solved.T, arrow_solved)
    arrow_total = lax.psum(arrow_local, ("tm", "col"))
    arrowhead = arrow_block - arrow_total
    return (
        day_factor,
        left_solved.reshape(left_coupling.shape),
        right_solved.reshape(right_coupling.shape),
        arrow_solved.reshape(arrow_coupling.shape),
        separator.reshape(separator_block.shape),
        arrowhead,
    )


def solution(mesh):
    return jax.shard_map(
        per_device,
        mesh=mesh,
        in_specs=(
            P("tm", None, "col", None, None, "row", None),
            P("tm", None, "col", None, None, "row", None),
            P("tm", None, "col", None, None, "row", None),
            P("tm", None, "col", None, None, "row", None),
            P("tm", None, "col", None, None),
            P(),
        ),
        out_specs=(
            P("tm", None, "col", None, None, "row", None),
            P("tm", None, "col", None, None, "row", None),
            P("tm", None, "col", None, None, "row", None),
            P("tm", None, "col", None, None),
            P("tm", None, "col", None, None, "row", None),
            P(),
        ),
        check_vma=False,
    )
```

profile of v0, /device:TPU:4, one launch (start us, length us, event | category | flops | bytes accessed | tf_op | source)
XLA Modules:
  0.0 1516.8 jit_solution(10383593552836481364)
XLA Ops:
  8.8 43.1 %all-gather.49.cloned.1.call-done = f32[1,1,1,512,4,1,128]{6,4,5,2,1,0,3:T(4,128)} async-done(((f32[1,1,1,32,4,1,128]{6,4,5,2,1,0,3:T(4,128)}), f32[1,1,1,512,4,1,128]{6,4,5,2,1,0,3:T(4,128)}) %all-gather.49.cloned.1.call-update) | async-done | bytes 1048592 | tf_op jit(solution)/shard_map/all_gather | solution.py:60
  56.8 21.8 %all-gather.39.cloned.1.call-done = f32[512,4,128]{2,0,1:T(8,128)} async-done(((f32[512,1,128]{2,0,1:T(8,128)}), f32[512,4,128]{2,0,1:T(8,128)}) %all-gather.39.cloned.1.call-update) | async-done | bytes 1048592 | tf_op jit(solution)/shard_map/all_gather | solution.py:65
  81.7 11.7 cholesky.462
  105.9 11.7 cholesky.481
  117.7 10.2 custom-call.36
  129.5 11.7 cholesky.502
  153.1 11.9 cholesky.519
  177.1 39.3 %custom-call.38 = f32[4,128,128]{1,2,0:T(8,128)S(1)} custom-call(f32[4,128,128]{2,1,0:T(8,128)S(1)} %get-tuple-element.178), custom_call_target="InvertDiagBlocksLowerTriangular" | custom-call | tf_op jit(solution)/shard_map/triangular_solve/custom-call.3 | solution.py:19
  228.2 44.8 %all-gather.51.cloned.1.call-done = f32[512,3,512]{2,0,1:T(8,128)} async-done(((f32[512,3,128]{2,0,1:T(8,128)}), f32[512,3,512]{2,0,1:T(8,128)}) %all-gather.51.cloned.1.call-update) | async-done | bytes 3145744 | tf_op jit(solution)/shard_map/all_gather | solution.py:74
  278.2 19.6 %all-gather.2 = f32[1,512,3,128]{3,1,2,0:T(8,128)S(1)} all-gather(f32[1,32,3,128]{3,1,2,0:T(8,128)S(1)} %slice.678), channel_id=4, replica_groups=mesh['tm'=4,'row'=4,'col'=16] {'col'}, dimensions={1}, use_global_device_ids=true | all-gather | bytes 835584 | tf_op jit(solution)/shard_map/all_gather | solution.py:60
  299.9 23.1 %all-gather.41.cloned.1.call-done = f32[512,4,128]{2,0,1:T(8,128)} async-done(((f32[512,1,128]{2,0,1:T(8,128)}), f32[512,4,128]{2,0,1:T(8,128)}) %all-gather.41.cloned.1.call-update) | async-done | bytes 1048592 | tf_op jit(solution)/shard_map/all_gather | solution.py:65
  328.3 11.7 cholesky.534
  353.1 11.7 cholesky.553
  377.3 11.7 cholesky.574
  401.0 11.9 cholesky.591
  417.3 11.6 while.21
  428.9 39.3 %custom-call.42 = f32[4,128,128]{1,2,0:T(8,128)S(1)} custom-call(f32[4,128,128]{2,1,0:T(8,128)S(1)} %get-tuple-element.179), custom_call_target="InvertDiagBlocksLowerTriangular" | custom-call | tf_op jit(solution)/shard_map/triangular_solve/custom-call.3 | solution.py:19
  485.7 32.4 %all-gather.53.cloned.1.call-done = f32[512,2,512]{2,0,1:T(8,128)} async-done(((f32[512,2,128]{2,0,1:T(8,128)}), f32[512,2,512]{2,0,1:T(8,128)}) %all-gather.53.cloned.1.call-update) | async-done | bytes 2097168 | tf_op jit(solution)/shard_map/all_gather | solution.py:74
  523.1 19.0 %all-gather.4 = f32[1,512,2,128]{3,1,2,0:T(8,128)S(1)} all-gather(f32[1,32,2,128]{3,1,2,0:T(8,128)S(1)} %slice.689), channel_id=6, replica_groups=mesh['tm'=4,'row'=4,'col'=16] {'col'}, dimensions={1}, use_global_device_ids=true | all-gather | bytes 557056 | tf_op jit(solution)/shard_map/all_gather | solution.py:60
  543.7 16.5 %all-gather.59.cloned.1.call-done = f32[1,1,1,512,4,1,128]{6,4,5,2,1,0,3:T(4,128)} async-done(((f32[1,1,1,32,4,1,128]{6,4,5,2,1,0,3:T(4,128)}), f32[1,1,1,512,4,1,128]{6,4,5,2,1,0,3:T(4,128)}) %all-gather.59.cloned.1.call-update) | async-done | bytes 1048592 | tf_op jit(solution)/shard_map/all_gather | solution.py:61
  571.5 27.8 %all-gather.67.cloned.1.call-done = f32[1,1,1,512,4,1,128]{6,4,5,2,1,0,3:T(4,128)} async-done(((f32[1,1,1,32,4,1,128]{6,4,5,2,1,0,3:T(4,128)}), f32[1,1,1,512,4,1,128]{6,4,5,2,1,0,3:T(4,128)}) %all-gather.67.cloned.1.call-update) | async-done | bytes 1048592 | tf_op jit(solution)/shard_map/all_gather | solution.py:62
  610.8 15.2 %all-gather.43.cloned.1.call-done = f32[512,4,128]{2,0,1:T(8,128)} async-done(((f32[512,1,128]{2,0,1:T(8,128)}), f32[512,4,128]{2,0,1:T(8,128)}) %all-gather.43.cloned.1.call-update) | async-done | bytes 1048592 | tf_op jit(solution)/shard_map/all_gather | solution.py:65
  631.1 11.7 cholesky.606
  656.7 11.7 cholesky.625
  681.5 11.7 cholesky.646
  705.2 11.9 cholesky.663
  721.4 11.5 while.22
  732.9 39.3 %custom-call.46 = f32[4,128,128]{1,2,0:T(8,128)S(1)} custom-call(f32[4,128,128]{2,1,0:T(8,128)S(1)} %get-tuple-element.180), custom_call_target="InvertDiagBlocksLowerTriangular" | custom-call | tf_op jit(solution)/shard_map/triangular_solve/custom-call.3 | solution.py:19
  815.3 19.6 %all-gather.6 = f32[1,512,1,128]{3,1,2,0:T(8,128)} all-gather(f32[1,32,1,128]{3,1,2,0:T(8,128)S(1)} %fusion.15), channel_id=8, replica_groups=mesh['tm'=4,'row'=4,'col'=16] {'col'}, dimensions={1}, use_global_device_ids=true | all-gather | bytes 278528 | tf_op jit(solution)/shard_map/all_gather | solution.py:60
  835.0 18.0 %all-gather.63.cloned.1.call-done = f32[1,512,4,128]{3,1,2,0:T(8,128)} async-done(((f32[1,32,4,128]{3,1,2,0:T(8,128)}), f32[1,512,4,128]{3,1,2,0:T(8,128)}) %all-gather.63.cloned.1.call-update) | async-done | bytes 1048592 | tf_op jit(solution)/shard_map/all_gather | solution.py:61
  868.1 24.0 %all-gather.71.cloned.1.call-done = f32[1,512,4,128]{3,1,2,0:T(8,128)} async-done(((f32[1,32,4,128]{3,1,2,0:T(8,128)}), f32[1,512,4,128]{3,1,2,0:T(8,128)}) %all-gather.71.cloned.1.call-update) | async-done | bytes 1048592 | tf_op jit(solution)/shard_map/all_gather | solution.py:62
  904.6 13.5 all-gather.57.cloned.1.call-done
  923.3 11.7 cholesky.678
  935.7 10.4 custom-call.47
  951.0 13.2 cholesky.697
  966.3 11.5 custom-call.48
  981.5 13.2 cholesky.718
  996.9 11.3 custom-call.49
  1011.1 13.6 cholesky.735
  1029.8 11.6 while.23
  1041.4 39.3 %custom-call.50 = f32[4,128,128]{1,2,0:T(8,128)S(1)} custom-call(f32[4,128,128]{2,1,0:T(8,128)S(1)} %get-tuple-element.181), custom_call_target="InvertDiagBlocksLowerTriangular" | custom-call | tf_op jit(solution)/shard_map/triangular_solve/custom-call.3 | solution.py:19
  1105.5 16.4 %all-gather.47.cloned.1.call-done = f32[128,4,4,128]{3,0,1,2:T(8,128)} async-done(((f32[128,4,1,128]{3,0,1,2:T(8,128)}), f32[128,4,4,128]{3,0,1,2:T(8,128)}) %all-gather.47.cloned.1.call-update) | async-done | bytes 1048592 | tf_op jit(solution)/shard_map/all_gather | solution.py:30
  1128.8 21.8 %all-gather.45.cloned.1.call-done = f32[128,4,4,128]{3,0,1,2:T(8,128)} async-done(((f32[128,4,1,128]{3,0,1,2:T(8,128)}), f32[128,4,4,128]{3,0,1,2:T(8,128)}) %all-gather.45.cloned.1.call-update) | async-done | bytes 1048592 | tf_op jit(solution)/shard_map/all_gather | solution.py:30
  1157.9 18.1 %all-gather.16 = f32[1,1,1,512,64]{4,3,2,1,0:T(8,128)S(1)} all-gather(f32[1,1,1,32,64]{4,3,2,1,0:T(8,128)S(1)} %slice-done.1), channel_id=18, replica_groups=mesh['tm'=4,'row'=4,'col'=16] {'col'}, dimensions={3}, use_global_device_ids=true | all-gather | bytes 139264 | tf_op jit(solution)/shard_map/all_gather | solution.py:63
  1185.0 16.1 %all-gather.17 = f32[1,512,64]{2,1,0:T(8,128)S(1)} all-gather(f32[1,32,64]{2,1,0:T(8,128)S(1)} %slice.716), channel_id=19, replica_groups=mesh['tm'=4,'row'=4,'col'=16] {'col'}, dimensions={1}, use_global_device_ids=true | all-gather | bytes 139264 | tf_op jit(solution)/shard_map/all_gather | solution.py:63
  1206.7 16.0 %all-gather.18 = f32[1,512,64]{2,1,0:T(8,128)S(1)} all-gather(f32[1,32,64]{2,1,0:T(8,128)S(1)} %slice.718), channel_id=20, replica_groups=mesh['tm'=4,'row'=4,'col'=16] {'col'}, dimensions={1}, use_global_device_ids=true | all-gather | bytes 139264 | tf_op jit(solution)/shard_map/all_gather | solution.py:63
  1228.6 15.9 %all-gather.19 = f32[1,512,64]{2,1,0:T(8,128)S(1)} all-gather(f32[1,32,64]{2,1,0:T(8,128)S(1)} %fusion.13), channel_id=21, replica_groups=mesh['tm'=4,'row'=4,'col'=16] {'col'}, dimensions={1}, use_global_device_ids=true | all-gather | bytes 139264 | tf_op jit(solution)/shard_map/all_gather | solution.py:63
  1247.9 249.4 %psum.7 = f32[64,64]{1,0:T(8,128)S(1)} all-reduce(f32[64,64]{1,0:T(8,128)S(1)} %convolution_bitcast_fusion), channel_id=1, replica_groups=mesh['tm'=4,'row'=4,'col'=16] {'tm','col'}, use_global_device_ids=true, to_apply=%region_10.0 | all-reduce | flops 4096 | bytes 32768 | tf_op jit(solution)/shard_map/psum | solution.py:129
  (494 shorter events, 412.3 us)
Async XLA Ops:
  7.2 44.7 %all-gather.49.cloned.1.call-start = ((), (), s32[]{:S(2)}) async-start(), calls=%async_computation.9 | async-start | bytes 1114112 | tf_op jit(solution)/shard_map/all_gather | solution.py:60
  8.7 69.9 %all-gather.39.cloned.1.call-start = ((), (), s32[]{:S(2)}) async-start(), calls=%async_computation.2 | async-start | bytes 1310720 | tf_op jit(solution)/shard_map/all_gather | solution.py:65
  54.0 218.9 %all-gather.51.cloned.1.call-start = ((), (), s32[]{:S(2)}) async-start(), calls=%async_computation.10 | async-start | bytes 3932160 | tf_op jit(solution)/shard_map/all_gather | solution.py:74
  219.4 379.8 %copy-start = (f32[128,512]{1,0:T(8,128)}, f32[128,512]{1,0:T(8,128)S(1)}, u32[]{:S(2)}) copy-start(f32[128,512]{1,0:T(8,128)S(1)} %fusion.151) | copy-start | bytes 786436
  221.5 53.7 %copy-start.11 = (f32[128,512]{1,0:T(8,128)}, f32[128,512]{1,0:T(8,128)S(1)}, u32[]{:S(2)}) copy-start(f32[128,512]{1,0:T(8,128)S(1)} %fusion.150) | copy-start | bytes 786436
  226.7 96.3 %all-gather.41.cloned.1.call-start = ((), (), s32[]{:S(2)}) async-start(), calls=%async_computation.3 | async-start | bytes 1310720 | tf_op jit(solution)/shard_map/all_gather | solution.py:65
  276.6 328.2 %copy-start.9 = (f32[512,3,32]{0,2,1:T(8,128)}, f32[512,3,32]{0,2,1:T(8,128)S(1)}, u32[]{:S(2)}) copy-start(f32[512,3,32]{0,2,1:T(8,128)S(1)} %copy.124) | copy-start | bytes 589828
  298.5 219.6 %all-gather.53.cloned.1.call-start = ((), (), s32[]{:S(2)}) async-start(), calls=%async_computation.11 | async-start | bytes 2621440 | tf_op jit(solution)/shard_map/all_gather | solution.py:74
  472.1 48.0 %copy-start.2 = (f32[128,512]{1,0:T(8,128)}, f32[128,512]{1,0:T(8,128)S(1)}, u32[]{:S(2)}) copy-start(f32[128,512]{1,0:T(8,128)S(1)} %fusion.145) | copy-start | bytes 786436
  479.6 80.6 %copy-start.12 = (f32[128,512]{1,0:T(8,128)S(1)}, f32[128,512]{1,0:T(8,128)}, u32[]{:S(2)}) copy-start(f32[128,512]{1,0:T(8,128)} %copy-done.11) | copy-start | bytes 786436
  480.5 79.7 %all-gather.59.cloned.1.call-start = ((), (), s32[]{:S(2)}) async-start(), calls=%async_computation.14 | async-start | bytes 1114112 | tf_op jit(solution)/shard_map/all_gather | solution.py:61
  482.0 117.2 %all-gather.67.cloned.1.call-start = ((), (), s32[]{:S(2)}) async-start(), calls=%async_computation.18 | async-start | bytes 1114112 | tf_op jit(solution)/shard_map/all_gather | solution.py:62
  483.6 142.4 %all-gather.43.cloned.1.call-start = ((), (), s32[]{:S(2)}) async-start(), calls=%async_computation.4 | async-start | bytes 1310720 | tf_op jit(solution)/shard_map/all_gather | solution.py:65
  520.1 46.6 %slice-start = ((f32[1,4,1,32,4,1,128]{6,5,4,3,2,1,0:T(1,128)}), f32[1,3,1,32,4,1,128]{6,5,4,3,2,1,0:T(1,128)S(1)}, s32[]{:S(2)}) async-start(f32[1,4,1,32,4,1,128]{6,5,4,3,2,1,0:T(1,128)} %param.34), calls=%async_computation.22 | async-start | bytes 393216 | tf_op jit(solution)/shard_map/slice.420
  523.0 46.1 %copy-start.57 = (f32[2,32,2,128]{3,1,2,0:T(8,128)}, f32[2,32,2,128]{3,1,2,0:T(8,128)S(1)}, u32[]{:S(2)}) copy-start(f32[2,32,2,128]{3,1,2,0:T(8,128)S(1)} %fusion.9) | copy-start | bytes 196612
  543.6 240.8 %all-gather.61.cloned.1.call-start = ((), (), s32[]{:S(2)}) async-start(), calls=%async_computation.15 | async-start | bytes 1114112 | tf_op jit(solution)/shard_map/all_gather | solution.py:61
  569.8 227.9 %all-gather.69.cloned.1.call-start = ((), (), s32[]{:S(2)}) async-start(), calls=%async_computation.19 | async-start | bytes 1114112 | tf_op jit(solution)/shard_map/all_gather | solution.py:62
  608.3 203.2 %all-gather.55.cloned.1.call-start = ((), (), s32[]{:S(2)}) async-start(), calls=%async_computation.12 | async-start | bytes 1310720 | tf_op jit(solution)/shard_map/all_gather | solution.py:74
  774.3 120.3 %copy-start.5 = (f32[128,512]{1,0:T(8,128)}, f32[128,512]{1,0:T(8,128)S(1)}, u32[]{:S(2)}) copy-start(f32[128,512]{1,0:T(8,128)S(1)} %fusion.141) | copy-start | bytes 786436
  777.1 117.6 %copy-start.17 = (f32[128,512]{1,0:T(8,128)}, f32[128,512]{1,0:T(8,128)S(1)}, u32[]{:S(2)}) copy-start(f32[128,512]{1,0:T(8,128)S(1)} %fusion.139) | copy-start | bytes 786436
  784.3 68.7 %all-gather.63.cloned.1.call-start = ((), (), s32[]{:S(2)}) async-start(), calls=%async_computation.16 | async-start | bytes 1114112 | tf_op jit(solution)/shard_map/all_gather | solution.py:61
  797.2 94.9 %all-gather.71.cloned.1.call-start = ((), (), s32[]{:S(2)}) async-start(), calls=%async_computation.20 | async-start | bytes 1114112 | tf_op jit(solution)/shard_map/all_gather | solution.py:62
  804.3 51.2 %copy-start.29 = (f32[128,512]{1,0:T(8,128)S(1)}, f32[128,512]{1,0:T(8,128)}, u32[]{:S(2)}) copy-start(f32[128,512]{1,0:T(8,128)} %copy-done.28) | copy-start | bytes 786436
  809.3 50.4 %copy-start.45 = (f32[2,32,4,128]{3,1,2,0:T(8,128)}, f32[2,32,4,128]{3,1,2,0:T(8,128)S(1)}, u32[]{:S(2)}) copy-start(f32[2,32,4,128]{3,1,2,0:T(8,128)S(1)} %fusion.3) | copy-start | bytes 393220
  810.0 108.1 %all-gather.57.cloned.1.call-start = ((), (), s32[]{:S(2)}) async-start(), calls=%async_computation.13 | async-start | bytes 1310720 | tf_op jit(solution)/shard_map/all_gather | solution.py:65
  814.0 48.1 %copy-start.47 = (f32[2,32,4,128]{3,1,2,0:T(8,128)S(1)}, f32[2,32,4,128]{3,1,2,0:T(8,128)}, u32[]{:S(2)}) copy-start(f32[2,32,4,128]{3,1,2,0:T(8,128)} %copy-done.46) | copy-start | bytes 393220
  834.9 253.6 %all-gather.65.cloned.1.call-start = ((), (), s32[]{:S(2)}) async-start(), calls=%async_computation.17 | async-start | bytes 1114112 | tf_op jit(solution)/shard_map/all_gather | solution.py:61
  865.1 234.1 %all-gather.73.cloned.1.call-start = ((), (), s32[]{:S(2)}) async-start(), calls=%async_computation.21 | async-start | bytes 1114112 | tf_op jit(solution)/shard_map/all_gather | solution.py:62
  904.3 217.6 %all-gather.47.cloned.1.call-start = ((), (), s32[]{:S(2)}) async-start(), calls=%async_computation.7 | async-start | bytes 1310720 | tf_op jit(solution)/shard_map/all_gather | solution.py:30
  1094.8 55.9 %all-gather.45.cloned.1.call-start = ((), (), s32[]{:S(2)}) async-start(), calls=%async_computation.5 | async-start | bytes 1310720 | tf_op jit(solution)/shard_map/all_gather | solution.py:30
  1105.5 394.0 %reduce-scatter.5.cloned.1.call-start = ((), (), s32[]{:S(2)}) async-start(), calls=%async_computation.8 | async-start | bytes 4456448 | tf_op jit(solution)/shard_map/reduce_scatter | solution.py:34
  1128.6 375.0 %reduce-scatter.3.cloned.1.call-start = ((), (), s32[]{:S(2)}) async-start(), calls=%async_computation.6 | async-start | bytes 4456448 | tf_op jit(solution)/shard_map/reduce_scatter | solution.py:34
  1157.4 43.7 %copy-start.4 = (f32[128,512]{1,0:T(8,128)S(1)}, f32[128,512]{1,0:T(8,128)}, u32[]{:S(2)}) copy-start(f32[128,512]{1,0:T(8,128)} %copy-done.2) | copy-start | bytes 786436
  1157.4 43.7 %copy-start.16 = (f32[128,512]{1,0:T(8,128)S(1)}, f32[128,512]{1,0:T(8,128)}, u32[]{:S(2)}) copy-start(f32[128,512]{1,0:T(8,128)} %copy-done.14) | copy-start | bytes 786436
  1157.4 65.3 %copy-start.6 = (f32[128,512]{1,0:T(8,128)S(1)}, f32[128,512]{1,0:T(8,128)}, u32[]{:S(2)}) copy-start(f32[128,512]{1,0:T(8,128)} %copy-done.5) | copy-start | bytes 786436
  1157.4 65.3 %copy-start.18 = (f32[128,512]{1,0:T(8,128)S(1)}, f32[128,512]{1,0:T(8,128)}, u32[]{:S(2)}) copy-start(f32[128,512]{1,0:T(8,128)} %copy-done.17) | copy-start | bytes 786436
  1179.0 43.7 %copy-start.30 = (f32[128,512]{1,0:T(8,128)S(1)}, f32[128,512]{1,0:T(8,128)}, u32[]{:S(2)}) copy-start(f32[128,512]{1,0:T(8,128)} %copy-done.28) | copy-start | bytes 786436
  1179.0 65.6 %copy-start.8 = (f32[128,512]{1,0:T(8,128)S(1)}, f32[128,512]{1,0:T(8,128)}, u32[]{:S(2)}) copy-start(f32[128,512]{1,0:T(8,128)} %copy-done.7) | copy-start | bytes 786436
  1179.0 65.6 %copy-start.20 = (f32[128,512]{1,0:T(8,128)S(1)}, f32[128,512]{1,0:T(8,128)}, u32[]{:S(2)}) copy-start(f32[128,512]{1,0:T(8,128)} %copy-done.19) | copy-start | bytes 786436
  1179.0 65.6 %copy-start.32 = (f32[128,512]{1,0:T(8,128)S(1)}, f32[128,512]{1,0:T(8,128)}, u32[]{:S(2)}) copy-start(f32[128,512]{1,0:T(8,128)} %copy-done.31) | copy-start | bytes 786436
  1202.2 42.3 %copy-start.38 = (f32[1,512,1,128]{3,1,2,0:T(8,128)S(1)}, f32[1,512,1,128]{3,1,2,0:T(8,128)}, u32[]{:S(2)}) copy-start(f32[1,512,1,128]{3,1,2,0:T(8,128)} %all-gather.6) | copy-start | bytes 786436
  1202.2 43.3 %copy-start.62 = (s32[32]{0:T(128)S(1)}, s32[32]{0:T(128)}, u32[]{:S(2)}) copy-start(s32[32]{0:T(128)} %iota_add_fusion) | copy-start | bytes 388
  1202.3 43.3 %copy-start.63 = (s32[128]{0:T(128)S(1)}, s32[128]{0:T(128)}, u32[]{:S(2)}) copy-start(s32[128]{0:T(128)} %iota_add_fusion.1) | copy-start | bytes 1540
  1222.7 274.7 %copy-start.61 = (f32[64,64]{1,0:T(8,128)S(1)}, f32[64,64]{1,0:T(8,128)}, u32[]{:S(2)}) copy-start(f32[64,64]{1,0:T(8,128)} %param.38) | copy-start | bytes 49156
  1223.9 277.9 %copy-start.55 = (f32[1,1,1,32,4,1,128]{6,5,4,3,2,1,0:T(1,128)S(1)}, f32[1,1,1,32,4,1,128]{6,5,4,3,2,1,0:T(1,128)}, u32[]{:S(2)}) copy-start(f32[1,1,1,32,4,1,128]{6,5,4,3,2,1,0:T(1,128)} %stack.85) | copy-start | bytes 196612
  1223.9 278.9 %copy-start.54 = (f32[1,1,1,32,4,1,128]{6,5,4,3,2,1,0:T(1,128)S(1)}, f32[1,1,1,32,4,1,128]{6,5,4,3,2,1,0:T(1,128)}, u32[]{:S(2)}) copy-start(f32[1,1,1,32,4,1,128]{6,5,4,3,2,1,0:T(1,128)} %stack.90) | copy-start | bytes 196612
  1224.9 283.0 %copy-start.53 = (f32[1,4,1,32,4,1,128]{6,5,4,3,2,1,0:T(1,128)S(1)}, f32[1,4,1,32,4,1,128]{6,5,4,3,2,1,0:T(1,128)}, u32[]{:S(2)}) copy-start(f32[1,4,1,32,4,1,128]{6,5,4,3,2,1,0:T(1,128)} %param.36) | copy-start | bytes 786436
  1499.5 8.5 collective-permute-start
  (39 other events, 307.1 us)
Sparse Core Ops, SparseCore 0:
  10.4 41.4 all-gather.48
  54.3 24.2 all-gather.38
  226.8 46.1 all-gather.50
  298.6 24.3 all-gather.40
  480.6 37.4 all-gather.52
  520.3 39.7 all-gather.58
  562.0 37.2 all-gather.66
  601.6 24.2 all-gather.42
  627.8 40.1 all-gather.60
  669.7 37.3 all-gather.68
  784.4 27.0 all-gather.54
  813.2 39.7 all-gather.62
  854.9 37.1 all-gather.70
  893.8 24.2 all-gather.56
  919.8 40.2 all-gather.64
  961.8 37.0 all-gather.72
  1094.9 26.9 all-gather.46
  1123.6 27.0 all-gather.44
  1153.2 65.4 reduce-scatter.4
  1221.1 62.4 reduce-scatter.2
where the time goes:
time: 1530 us; the launch traced here: 1520 us
  other arithmetic  503 us (33%)
  blocking collectives  374 us (24%)
  waiting for transfers between devices  325 us (21%)
  local copies, waits for them, and re-layouts  159 us (10%)
  matrix products  126 us (8%)
  between operations  26.5 us (2%)
    another operation x59, other arithmetic, per_device(): factor = jnp.linalg.cholesky(diagonal_full)  329 us
    psum x1, blocking collectives, per_device(): arrow_total = lax.psum(arrow_local, ('tm', 'col'))  249 us
    another operation x9, other arithmetic, lower_inverse(): lax.linalg.triangular_solve(factor, identity, left_side=True, lower=True)  161 us
    all_gather x3, waiting for transfers between devices, per_device(): lax.all_gather(owned[:, 1:, None, :], 'row', axis=2, tiled=True)  78.6 us
    all_gather x4, waiting for transfers between devices, per_device(): lax.all_gather(gathered_day[:, 0:1, :], 'row', axis=1, tiled=True)  73.6 us
    dot_general x31, matrix products, product(): jnp.dot(left, right, precision=lax.Precision.HIGHEST, preferred_element_t...  73.6 us
    all_gather x4, blocking collectives, per_device(): lax.all_gather(arrow_part[current], 'col', axis=0, tiled=True)  66.2 us
    all_gather x3, blocking collectives, per_device(): lax.all_gather(matrix[current, :, current:, :], 'col', axis=0, tiled=True)  58.2 us
  transfers between devices with their start and end apart: 21, of which 15 were waited for; matrix products, arithmetic and copies ran while one was open for 31% of the time, Pallas kernels for 0%

commit v1 on v0

--- a/solution.py
+++ b/solution.py
@@ -126,7 +126,7 @@
     from_next = passed_along(left_term, "tm", -1)
     separator = separator_local - right_term - from_next
     arrow_local = product(arrow_solved.T, arrow_solved)
-    arrow_total = lax.psum(arrow_local, ("tm", "col"))
+    arrow_total = jnp.sum(lax.all_gather(arrow_local, ("tm", "col")), axis=0)
     arrowhead = arrow_block - arrow_total
     return (
         day_factor,

time: 1530 us -> 1380 us (0.902)
  blocking collectives: 374 us -> 124 us
  waiting for transfers between devices: 325 us -> 431 us
    psum x1 -> x0, blocking collectives: 249 us -> none  [per_device(): arrow_total = lax.psum(arrow_local, ('tm', 'col'))]
    all_gather x0 -> x1, waiting for transfers between devices: none -> 71.3 us  [per_device(): arrow_total = jnp.sum(lax.all_gather(arrow_local, ('tm', 'col')), axis=0)]
    reduce_scatter x2, waiting for transfers between devices: 0.01 us -> 61 us  [separator_term(): lax.psum_scatter(product(ordered, solved), 'col', scatter_dimension=0, ti...]
    all_gather x2, waiting for transfers between devices: 38.2 us -> 17 us  [separator_term(): lax.all_gather(solved.reshape(solved.shape[0], panels, 1, row_width), 'ro...]
  transfers between devices with their start and end apart: 21 -> 22, of which waited for: 15 -> 15; matrix products, arithmetic and copies ran while one was open for 31% -> 34% of each run, Pallas kernels for 0% -> 0%
where the time goes in v1:
time: 1380 us; the launch traced here: 1370 us
  other arithmetic  501 us (36%)
  waiting for transfers between devices  431 us (31%)
  local copies, waits for them, and re-layouts  157 us (11%)
  matrix products  125 us (9%)
  blocking collectives  124 us (9%)
  between operations  26.6 us (2%)
    another operation x59, other arithmetic, per_device(): factor = jnp.linalg.cholesky(diagonal_full)  329 us
    another operation x9, other arithmetic, lower_inverse(): lax.linalg.triangular_solve(factor, identity, left_side=True, lower=True)  161 us
    all_gather x3, waiting for transfers between devices, per_device(): lax.all_gather(owned[:, 1:, None, :], 'row', axis=2, tiled=True)  78.8 us
    dot_general x31, matrix products, product(): jnp.dot(left, right, precision=lax.Precision.HIGHEST, preferred_element_t...  73.8 us
    all_gather x4, waiting for transfers between devices, per_device(): lax.all_gather(gathered_day[:, 0:1, :], 'row', axis=1, tiled=True)  73.5 us
    all_gather x1, waiting for transfers between devices, per_device(): arrow_total = jnp.sum(lax.all_gather(arrow_local, ('tm', 'col')), axis=0)  71.3 us
    all_gather x4, blocking collectives, per_device(): lax.all_gather(arrow_part[current], 'col', axis=0, tiled=True)  65.8 us
    reduce_scatter x2, waiting for transfers between devices, separator_term(): lax.psum_scatter(product(ordered, solved), 'col', scatter_dimension=0, ti...  61 us
  transfers between devices with their start and end apart: 22, of which 15 were waited for; matrix products, arithmetic and copies ran while one was open for 34% of the time, Pallas kernels for 0%

profile of v1, /device:TPU:4, one launch (start us, length us, event | category | flops | bytes accessed | tf_op | source)
XLA Modules:
  0.0 1369.1 jit_solution(8451575155954148226)
XLA Ops:
  8.8 43.1 %all-gather.51.cloned.1.call-done = f32[1,1,1,512,4,1,128]{6,4,5,2,1,0,3:T(4,128)} async-done(((f32[1,1,1,32,4,1,128]{6,4,5,2,1,0,3:T(4,128)}), f32[1,1,1,512,4,1,128]{6,4,5,2,1,0,3:T(4,128)}) %all-gather.51.cloned.1.call-update) | async-done | bytes 1048592 | tf_op jit(solution)/shard_map/all_gather | solution.py:60
  56.8 21.8 %all-gather.41.cloned.1.call-done = f32[512,4,128]{2,0,1:T(8,128)} async-done(((f32[512,1,128]{2,0,1:T(8,128)}), f32[512,4,128]{2,0,1:T(8,128)}) %all-gather.41.cloned.1.call-update) | async-done | bytes 1048592 | tf_op jit(solution)/shard_map/all_gather | solution.py:65
  81.7 11.7 cholesky.462
  105.9 11.7 cholesky.481
  129.2 11.7 cholesky.502
  152.8 11.9 cholesky.519
  176.8 39.3 %custom-call.38 = f32[4,128,128]{1,2,0:T(8,128)S(1)} custom-call(f32[4,128,128]{2,1,0:T(8,128)S(1)} %get-tuple-element.178), custom_call_target="InvertDiagBlocksLowerTriangular" | custom-call | tf_op jit(solution)/shard_map/triangular_solve/custom-call.3 | solution.py:19
  228.0 44.8 %all-gather.53.cloned.1.call-done = f32[512,3,512]{2,0,1:T(8,128)} async-done(((f32[512,3,128]{2,0,1:T(8,128)}), f32[512,3,512]{2,0,1:T(8,128)}) %all-gather.53.cloned.1.call-update) | async-done | bytes 3145744 | tf_op jit(solution)/shard_map/all_gather | solution.py:74
  277.9 19.6 %all-gather.2 = f32[1,512,3,128]{3,1,2,0:T(8,128)S(1)} all-gather(f32[1,32,3,128]{3,1,2,0:T(8,128)S(1)} %slice.678), channel_id=4, replica_groups=mesh['tm'=4,'row'=4,'col'=16] {'col'}, dimensions={1}, use_global_device_ids=true | all-gather | bytes 835584 | tf_op jit(solution)/shard_map/all_gather | solution.py:60
  299.9 22.9 %all-gather.43.cloned.1.call-done = f32[512,4,128]{2,0,1:T(8,128)} async-done(((f32[512,1,128]{2,0,1:T(8,128)}), f32[512,4,128]{2,0,1:T(8,128)}) %all-gather.43.cloned.1.call-update) | async-done | bytes 1048592 | tf_op jit(solution)/shard_map/all_gather | solution.py:65
  328.0 11.7 cholesky.534
  352.9 11.7 cholesky.553
  376.8 11.7 cholesky.574
  400.5 12.1 cholesky.591
  416.9 11.6 while.21
  428.4 39.3 %custom-call.42 = f32[4,128,128]{1,2,0:T(8,128)S(1)} custom-call(f32[4,128,128]{2,1,0:T(8,128)S(1)} %get-tuple-element.179), custom_call_target="InvertDiagBlocksLowerTriangular" | custom-call | tf_op jit(solution)/shard_map/triangular_solve/custom-call.3 | solution.py:19
  484.6 32.4 %all-gather.55.cloned.1.call-done = f32[512,2,512]{2,0,1:T(8,128)} async-done(((f32[512,2,128]{2,0,1:T(8,128)}), f32[512,2,512]{2,0,1:T(8,128)}) %all-gather.55.cloned.1.call-update) | async-done | bytes 2097168 | tf_op jit(solution)/shard_map/all_gather | solution.py:74
  521.9 19.0 %all-gather.4 = f32[1,512,2,128]{3,1,2,0:T(8,128)S(1)} all-gather(f32[1,32,2,128]{3,1,2,0:T(8,128)S(1)} %slice.689), channel_id=6, replica_groups=mesh['tm'=4,'row'=4,'col'=16] {'col'}, dimensions={1}, use_global_device_ids=true | all-gather | bytes 557056 | tf_op jit(solution)/shard_map/all_gather | solution.py:60
  542.5 16.6 %all-gather.61.cloned.1.call-done = f32[1,1,1,512,4,1,128]{6,4,5,2,1,0,3:T(4,128)} async-done(((f32[1,1,1,32,4,1,128]{6,4,5,2,1,0,3:T(4,128)}), f32[1,1,1,512,4,1,128]{6,4,5,2,1,0,3:T(4,128)}) %all-gather.61.cloned.1.call-update) | async-done | bytes 1048592 | tf_op jit(solution)/shard_map/all_gather | solution.py:61
  570.5 27.7 %all-gather.69.cloned.1.call-done = f32[1,1,1,512,4,1,128]{6,4,5,2,1,0,3:T(4,128)} async-done(((f32[1,1,1,32,4,1,128]{6,4,5,2,1,0,3:T(4,128)}), f32[1,1,1,512,4,1,128]{6,4,5,2,1,0,3:T(4,128)}) %all-gather.69.cloned.1.call-update) | async-done | bytes 1048592 | tf_op jit(solution)/shard_map/all_gather | solution.py:62
  609.5 15.4 %all-gather.45.cloned.1.call-done = f32[512,4,128]{2,0,1:T(8,128)} async-done(((f32[512,1,128]{2,0,1:T(8,128)}), f32[512,4,128]{2,0,1:T(8,128)}) %all-gather.45.cloned.1.call-update) | async-done | bytes 1048592 | tf_op jit(solution)/shard_map/all_gather | solution.py:65
  630.1 11.7 cholesky.606
  655.7 11.7 cholesky.625
  668.1 10.0 custom-call.44
  680.6 11.7 cholesky.646
  704.3 12.1 cholesky.663
  720.7 12.0 while.22
  732.7 39.3 %custom-call.46 = f32[4,128,128]{1,2,0:T(8,128)S(1)} custom-call(f32[4,128,128]{2,1,0:T(8,128)S(1)} %get-tuple-element.180), custom_call_target="InvertDiagBlocksLowerTriangular" | custom-call | tf_op jit(solution)/shard_map/triangular_solve/custom-call.3 | solution.py:19
  814.3 19.7 %all-gather.6 = f32[1,512,1,128]{3,1,2,0:T(8,128)} all-gather(f32[1,32,1,128]{3,1,2,0:T(8,128)S(1)} %fusion.15), channel_id=8, replica_groups=mesh['tm'=4,'row'=4,'col'=16] {'col'}, dimensions={1}, use_global_device_ids=true | all-gather | bytes 278528 | tf_op jit(solution)/shard_map/all_gather | solution.py:60
  834.1 18.0 %all-gather.65.cloned.1.call-done = f32[1,512,4,128]{3,1,2,0:T(8,128)} async-done(((f32[1,32,4,128]{3,1,2,0:T(8,128)}), f32[1,512,4,128]{3,1,2,0:T(8,128)}) %all-gather.65.cloned.1.call-update) | async-done | bytes 1048592 | tf_op jit(solution)/shard_map/all_gather | solution.py:61
  867.2 24.0 %all-gather.73.cloned.1.call-done = f32[1,512,4,128]{3,1,2,0:T(8,128)} async-done(((f32[1,32,4,128]{3,1,2,0:T(8,128)}), f32[1,512,4,128]{3,1,2,0:T(8,128)}) %all-gather.73.cloned.1.call-update) | async-done | bytes 1048592 | tf_op jit(solution)/shard_map/all_gather | solution.py:62
  903.7 13.5 all-gather.59.cloned.1.call-done
  922.4 11.7 cholesky.678
  934.8 10.4 custom-call.47
  950.0 13.2 cholesky.697
  965.4 11.7 custom-call.48
  980.8 13.2 cholesky.718
  996.2 11.3 custom-call.49
  1010.4 13.3 cholesky.735
  1029.0 11.6 while.23
  1040.5 39.3 %custom-call.50 = f32[4,128,128]{1,2,0:T(8,128)S(1)} custom-call(f32[4,128,128]{2,1,0:T(8,128)S(1)} %get-tuple-element.181), custom_call_target="InvertDiagBlocksLowerTriangular" | custom-call | tf_op jit(solution)/shard_map/triangular_solve/custom-call.3 | solution.py:19
  1103.3 17.0 %all-gather.49.cloned.1.call-done = f32[128,4,4,128]{3,0,1,2:T(8,128)} async-done(((f32[128,4,1,128]{3,0,1,2:T(8,128)}), f32[128,4,4,128]{3,0,1,2:T(8,128)}) %all-gather.49.cloned.1.call-update) | async-done | bytes 1048592 | tf_op jit(solution)/shard_map/all_gather | solution.py:30
  1127.6 18.1 %all-gather.16 = f32[1,1,1,512,64]{4,3,2,1,0:T(8,128)S(1)} all-gather(f32[1,1,1,32,64]{4,3,2,1,0:T(8,128)S(1)} %slice-done.1), channel_id=18, replica_groups=mesh['tm'=4,'row'=4,'col'=16] {'col'}, dimensions={3}, use_global_device_ids=true | all-gather | bytes 139264 | tf_op jit(solution)/shard_map/all_gather | solution.py:63
  1149.0 15.7 %all-gather.17 = f32[1,512,64]{2,1,0:T(8,128)S(1)} all-gather(f32[1,32,64]{2,1,0:T(8,128)S(1)} %slice.716), channel_id=19, replica_groups=mesh['tm'=4,'row'=4,'col'=16] {'col'}, dimensions={1}, use_global_device_ids=true | all-gather | bytes 139264 | tf_op jit(solution)/shard_map/all_gather | solution.py:63
  1166.3 16.3 %all-gather.18 = f32[1,512,64]{2,1,0:T(8,128)S(1)} all-gather(f32[1,32,64]{2,1,0:T(8,128)S(1)} %slice.718), channel_id=20, replica_groups=mesh['tm'=4,'row'=4,'col'=16] {'col'}, dimensions={1}, use_global_device_ids=true | all-gather | bytes 139264 | tf_op jit(solution)/shard_map/all_gather | solution.py:63
  1185.0 15.7 %all-gather.19 = f32[1,512,64]{2,1,0:T(8,128)S(1)} all-gather(f32[1,32,64]{2,1,0:T(8,128)S(1)} %fusion.13), channel_id=21, replica_groups=mesh['tm'=4,'row'=4,'col'=16] {'col'}, dimensions={1}, use_global_device_ids=true | all-gather | bytes 139264 | tf_op jit(solution)/shard_map/all_gather | solution.py:63
  1225.4 71.3 %all-gather.77.cloned.1.call-done = f32[4096,64]{1,0:T(8,128)} async-done(((f32[64,64]{1,0:T(8,128)}), f32[4096,64]{1,0:T(8,128)}) %all-gather.77.cloned.1.call-update) | async-done | bytes 1048592 | tf_op jit(solution)/shard_map/all_gather | solution.py:129
  1299.1 61.0 %reduce-scatter.3.cloned.1.call-done = f32[128,512]{1,0:T(8,128)} async-done(((f32[2048,512]{1,0:T(8,128)}), f32[128,512]{1,0:T(8,128)}) %reduce-scatter.3.cloned.1.call-update) | async-done | bytes 262160 | tf_op jit(solution)/shard_map/reduce_scatter | solution.py:34
  (503 shorter events, 403.2 us)
Async XLA Ops:
  7.2 44.7 %all-gather.51.cloned.1.call-start = ((), (), s32[]{:S(2)}) async-start(), calls=%async_computation.9 | async-start | bytes 1114112 | tf_op jit(solution)/shard_map/all_gather | solution.py:60
  8.7 69.9 %all-gather.41.cloned.1.call-start = ((), (), s32[]{:S(2)}) async-start(), calls=%async_computation.2 | async-start | bytes 1310720 | tf_op jit(solution)/shard_map/all_gather | solution.py:65
  54.0 218.7 %all-gather.53.cloned.1.call-start = ((), (), s32[]{:S(2)}) async-start(), calls=%async_computation.10 | async-start | bytes 3932160 | tf_op jit(solution)/shard_map/all_gather | solution.py:74
  176.8 39.8 %copy-start.23 = (f32[512,512]{1,0:T(8,128)}, f32[512,512]{1,0:T(8,128)S(1)}, u32[]{:S(2)}) copy-start(f32[512,512]{1,0:T(8,128)S(1)} %get-tuple-element.506) | copy-start | bytes 3145732
  219.2 379.0 %copy-start = (f32[128,512]{1,0:T(8,128)}, f32[128,512]{1,0:T(8,128)S(1)}, u32[]{:S(2)}) copy-start(f32[128,512]{1,0:T(8,128)S(1)} %fusion.151) | copy-start | bytes 786436
  226.4 96.3 %all-gather.43.cloned.1.call-start = ((), (), s32[]{:S(2)}) async-start(), calls=%async_computation.3 | async-start | bytes 1310720 | tf_op jit(solution)/shard_map/all_gather | solution.py:65
  276.4 327.5 %copy-start.9 = (f32[512,3,32]{0,2,1:T(8,128)}, f32[512,3,32]{0,2,1:T(8,128)S(1)}, u32[]{:S(2)}) copy-start(f32[512,3,32]{0,2,1:T(8,128)S(1)} %copy.124) | copy-start | bytes 589828
  298.2 218.7 %all-gather.55.cloned.1.call-start = ((), (), s32[]{:S(2)}) async-start(), calls=%async_computation.11 | async-start | bytes 2621440 | tf_op jit(solution)/shard_map/all_gather | solution.py:74
  479.3 79.8 %copy-start.12 = (f32[128,512]{1,0:T(8,128)S(1)}, f32[128,512]{1,0:T(8,128)}, u32[]{:S(2)}) copy-start(f32[128,512]{1,0:T(8,128)} %copy-done.11) | copy-start | bytes 786436
  479.4 79.7 %all-gather.61.cloned.1.call-start = ((), (), s32[]{:S(2)}) async-start(), calls=%async_computation.14 | async-start | bytes 1114112 | tf_op jit(solution)/shard_map/all_gather | solution.py:61
  480.9 117.3 %all-gather.69.cloned.1.call-start = ((), (), s32[]{:S(2)}) async-start(), calls=%async_computation.18 | async-start | bytes 1114112 | tf_op jit(solution)/shard_map/all_gather | solution.py:62
  482.5 142.4 %all-gather.45.cloned.1.call-start = ((), (), s32[]{:S(2)}) async-start(), calls=%async_computation.4 | async-start | bytes 1310720 | tf_op jit(solution)/shard_map/all_gather | solution.py:65
  521.9 43.9 %copy-start.64 = (f32[2,32,2,128]{3,1,2,0:T(8,128)}, f32[2,32,2,128]{3,1,2,0:T(8,128)S(1)}, u32[]{:S(2)}) copy-start(f32[2,32,2,128]{3,1,2,0:T(8,128)S(1)} %fusion.9) | copy-start | bytes 196612
  541.7 24.1 %slice-start = ((f32[1,4,1,32,4,1,128]{6,5,4,3,2,1,0:T(1,128)}), f32[1,3,1,32,4,1,128]{6,5,4,3,2,1,0:T(1,128)S(1)}, s32[]{:S(2)}) async-start(f32[1,4,1,32,4,1,128]{6,5,4,3,2,1,0:T(1,128)} %param.34), calls=%async_computation.23 | async-start | bytes 393216 | tf_op jit(solution)/shard_map/slice.420
  542.5 241.0 %all-gather.63.cloned.1.call-start = ((), (), s32[]{:S(2)}) async-start(), calls=%async_computation.15 | async-start | bytes 1114112 | tf_op jit(solution)/shard_map/all_gather | solution.py:61
  568.1 34.1 %copy-start.42 = (f32[3,32,4,128]{3,1,2,0:T(8,128)}, f32[3,32,4,128]{3,1,2,0:T(8,128)S(1)}, u32[]{:S(2)}) copy-start(f32[3,32,4,128]{3,1,2,0:T(8,128)S(1)} %fusion) | copy-start | bytes 589828
  568.8 227.7 %all-gather.71.cloned.1.call-start = ((), (), s32[]{:S(2)}) async-start(), calls=%async_computation.19 | async-start | bytes 1114112 | tf_op jit(solution)/shard_map/all_gather | solution.py:62
  607.2 203.3 %all-gather.57.cloned.1.call-start = ((), (), s32[]{:S(2)}) async-start(), calls=%async_computation.12 | async-start | bytes 1310720 | tf_op jit(solution)/shard_map/all_gather | solution.py:74
  774.1 119.6 %copy-start.5 = (f32[128,512]{1,0:T(8,128)}, f32[128,512]{1,0:T(8,128)S(1)}, u32[]{:S(2)}) copy-start(f32[128,512]{1,0:T(8,128)S(1)} %fusion.141) | copy-start | bytes 786436
  776.0 117.7 %copy-start.17 = (f32[128,512]{1,0:T(8,128)}, f32[128,512]{1,0:T(8,128)S(1)}, u32[]{:S(2)}) copy-start(f32[128,512]{1,0:T(8,128)S(1)} %fusion.139) | copy-start | bytes 786436
  783.4 68.7 %all-gather.65.cloned.1.call-start = ((), (), s32[]{:S(2)}) async-start(), calls=%async_computation.16 | async-start | bytes 1114112 | tf_op jit(solution)/shard_map/all_gather | solution.py:61
  796.3 94.9 %all-gather.73.cloned.1.call-start = ((), (), s32[]{:S(2)}) async-start(), calls=%async_computation.20 | async-start | bytes 1114112 | tf_op jit(solution)/shard_map/all_gather | solution.py:62
  805.8 48.9 %copy-start.29 = (f32[128,512]{1,0:T(8,128)S(1)}, f32[128,512]{1,0:T(8,128)}, u32[]{:S(2)}) copy-start(f32[128,512]{1,0:T(8,128)} %copy-done.28) | copy-start | bytes 786436
  808.1 50.6 %copy-start.48 = (f32[2,32,4,128]{3,1,2,0:T(8,128)}, f32[2,32,4,128]{3,1,2,0:T(8,128)S(1)}, u32[]{:S(2)}) copy-start(f32[2,32,4,128]{3,1,2,0:T(8,128)S(1)} %fusion.3) | copy-start | bytes 393220
  808.8 108.3 %all-gather.59.cloned.1.call-start = ((), (), s32[]{:S(2)}) async-start(), calls=%async_computation.13 | async-start | bytes 1310720 | tf_op jit(solution)/shard_map/all_gather | solution.py:65
  834.1 253.6 %all-gather.67.cloned.1.call-start = ((), (), s32[]{:S(2)}) async-start(), calls=%async_computation.17 | async-start | bytes 1114112 | tf_op jit(solution)/shard_map/all_gather | solution.py:61
  864.2 233.3 %all-gather.75.cloned.1.call-start = ((), (), s32[]{:S(2)}) async-start(), calls=%async_computation.21 | async-start | bytes 1114112 | tf_op jit(solution)/shard_map/all_gather | solution.py:62
  903.4 216.8 %all-gather.49.cloned.1.call-start = ((), (), s32[]{:S(2)}) async-start(), calls=%async_computation.7 | async-start | bytes 1310720 | tf_op jit(solution)/shard_map/all_gather | solution.py:30
  1093.1 109.6 %all-gather.47.cloned.1.call-start = ((), (), s32[]{:S(2)}) async-start(), calls=%async_computation.5 | async-start | bytes 1310720 | tf_op jit(solution)/shard_map/all_gather | solution.py:30
  1102.0 19.9 %copy-start.37 = (f32[4,32,512]{2,1,0:T(8,128)S(1)}, f32[4,32,512]{2,1,0:T(8,128)}, u32[]{:S(2)}) copy-start(f32[4,32,512]{2,1,0:T(8,128)} %copy-done.36) | copy-start | bytes 786436
  1102.1 19.8 %copy-start.34 = (f32[4,32,512]{2,1,0:T(8,128)}, f32[4,32,512]{2,1,0:T(8,128)S(1)}, u32[]{:S(2)}) copy-start(f32[4,32,512]{2,1,0:T(8,128)S(1)} %pad_maximum_fusion.6) | copy-start | bytes 786436
  1103.0 118.3 %reduce-scatter.5.cloned.1.call-start = ((), (), s32[]{:S(2)}) async-start(), calls=%async_computation.8 | async-start | bytes 4456448 | tf_op jit(solution)/shard_map/reduce_scatter | solution.py:34
  1126.9 18.8 %copy-start.1 = (f32[128,512]{1,0:T(8,128)S(1)}, f32[128,512]{1,0:T(8,128)}, u32[]{:S(2)}) copy-start(f32[128,512]{1,0:T(8,128)} %copy-done) | copy-start | bytes 786436
  1126.9 18.8 %copy-start.13 = (f32[128,512]{1,0:T(8,128)S(1)}, f32[128,512]{1,0:T(8,128)}, u32[]{:S(2)}) copy-start(f32[128,512]{1,0:T(8,128)} %copy-done.11) | copy-start | bytes 786436
  1126.9 20.8 %copy-start.10 = (f32[512,3,32]{0,2,1:T(8,128)S(1)}, f32[512,3,32]{0,2,1:T(8,128)}, u32[]{:S(2)}) copy-start(f32[512,3,32]{0,2,1:T(8,128)} %copy-done.9) | copy-start | bytes 589828
  1126.9 37.9 %copy-start.4 = (f32[128,512]{1,0:T(8,128)S(1)}, f32[128,512]{1,0:T(8,128)}, u32[]{:S(2)}) copy-start(f32[128,512]{1,0:T(8,128)} %copy-done.2) | copy-start | bytes 786436
  1126.9 37.9 %copy-start.16 = (f32[128,512]{1,0:T(8,128)S(1)}, f32[128,512]{1,0:T(8,128)}, u32[]{:S(2)}) copy-start(f32[128,512]{1,0:T(8,128)} %copy-done.14) | copy-start | bytes 786436
  1126.9 55.7 %copy-start.6 = (f32[128,512]{1,0:T(8,128)S(1)}, f32[128,512]{1,0:T(8,128)}, u32[]{:S(2)}) copy-start(f32[128,512]{1,0:T(8,128)} %copy-done.5) | copy-start | bytes 786436
  1127.0 55.7 %copy-start.18 = (f32[128,512]{1,0:T(8,128)S(1)}, f32[128,512]{1,0:T(8,128)}, u32[]{:S(2)}) copy-start(f32[128,512]{1,0:T(8,128)} %copy-done.17) | copy-start | bytes 786436
  1127.0 169.8 %all-gather.77.cloned.1.call-start = ((), (), s32[]{:S(2)}) async-start(), calls=%async_computation.22 | async-start | bytes 2129920 | tf_op jit(solution)/shard_map/all_gather | solution.py:129
  1147.6 35.1 %copy-start.30 = (f32[128,512]{1,0:T(8,128)S(1)}, f32[128,512]{1,0:T(8,128)}, u32[]{:S(2)}) copy-start(f32[128,512]{1,0:T(8,128)} %copy-done.28) | copy-start | bytes 786436
  1147.6 53.2 %copy-start.8 = (f32[128,512]{1,0:T(8,128)S(1)}, f32[128,512]{1,0:T(8,128)}, u32[]{:S(2)}) copy-start(f32[128,512]{1,0:T(8,128)} %copy-done.7) | copy-start | bytes 786436
  1147.6 53.2 %copy-start.20 = (f32[128,512]{1,0:T(8,128)S(1)}, f32[128,512]{1,0:T(8,128)}, u32[]{:S(2)}) copy-start(f32[128,512]{1,0:T(8,128)} %copy-done.19) | copy-start | bytes 786436
  1147.6 53.2 %copy-start.32 = (f32[128,512]{1,0:T(8,128)S(1)}, f32[128,512]{1,0:T(8,128)}, u32[]{:S(2)}) copy-start(f32[128,512]{1,0:T(8,128)} %copy-done.31) | copy-start | bytes 786436
  1202.7 157.5 %reduce-scatter.3.cloned.1.call-start = ((), (), s32[]{:S(2)}) async-start(), calls=%async_computation.6 | async-start | bytes 4456448 | tf_op jit(solution)/shard_map/reduce_scatter | solution.py:34
  1217.7 80.8 %copy-start.66 = (f32[64,64]{1,0:T(8,128)S(1)}, f32[64,64]{1,0:T(8,128)}, u32[]{:S(2)}) copy-start(f32[64,64]{1,0:T(8,128)} %param.38) | copy-start | bytes 49156
  1217.7 142.5 %copy-start.56 = (f32[1,4,1,32,4,1,128]{6,5,4,3,2,1,0:T(1,128)S(1)}, f32[1,4,1,32,4,1,128]{6,5,4,3,2,1,0:T(1,128)}, u32[]{:S(2)}) copy-start(f32[1,4,1,32,4,1,128]{6,5,4,3,2,1,0:T(1,128)} %param.36) | copy-start | bytes 786436
  1221.3 138.9 %collective-permute-start = (f32[128,512]{1,0:T(8,128)}, f32[128,512]{1,0:T(8,128)S(1)}, u32[]{:S(2)}, u32[]{:S(2)}) collective-permute-start(f32[128,512]{1,0:T(8,128)} %reduce-scatter.5.cloned.1.call-done), channel_id=1, source_target_pairs={{64,0},{128,64},{192,128},{65,1},{129,65},{193,129},{66,2},{130,66... | collective-permute-start | bytes 786440 | tf_op jit(solution)/shard_map/ppermute | solution.py:10
  (43 other events, 157.8 us)
Sparse Core Ops, SparseCore 0:
  10.4 41.4 all-gather.50
  54.3 24.2 all-gather.40
  226.5 46.1 all-gather.52
  298.3 24.3 all-gather.42
  479.5 37.4 all-gather.54
  519.2 39.8 all-gather.60
  560.9 37.2 all-gather.68
  600.6 24.2 all-gather.44
  626.7 40.1 all-gather.62
  668.6 37.2 all-gather.70
  783.5 27.0 all-gather.56
  812.3 39.7 all-gather.64
  853.9 37.1 all-gather.72
  892.8 24.2 all-gather.58
  918.9 40.2 all-gather.66
  960.9 37.0 all-gather.74
  1093.2 26.9 all-gather.48
  1121.9 27.0 all-gather.46
  1151.5 65.2 reduce-scatter.4
  1220.0 76.6 all-gather.76
  1299.3 60.8 reduce-scatter.2
